TPU v7x, 512 devices: a whole 4x4x16 slice. The times are simulated.
512 devices in a mesh: fsdp: 128 (over z, y, core), seq: 4 (over x).
Axes of the slice: x: 4, y: 4, z: 16, core: 2. Of those that a mesh axis runs over, the one named last changes fastest.
Arguments:
- tokens: bfloat16 [128, 512, 8192], P('fsdp', 'seq'), may hold values from -6 to 6
- queries: bfloat16 [128, 512, 8192], P('fsdp', None, 'seq'), may hold values from -6 to 6
- key_weight: bfloat16 [8192, 1024], P('fsdp', 'seq'), may hold values from -1 to 1
- u_factor: float32 [8192, 64], P('fsdp'), may hold values from -6 to 6
- v_factor: float32 [1024, 64], replicated, may hold values from -6 to 6
Outputs:
- update: float32 [8192, 1024], P('fsdp')
- losses: float32 [2], replicated
All inputs are finite; a program needn't handle non-finite values.
Results may differ from a plain program's by a relative error of at most 0.0003.
Values may be sent and summed in bfloat16 or wider, within the bound.
No kernel may reach another device: no remote copies, remote signals or barrier semaphores. Data moves between devices by JAX's collectives and lax.ppermute only.
A program may use at most 64 MiB of HBM per device.

v0:
```python
import math
import jax
import jax.numpy as jnp
from jax import lax
from jax.sharding import PartitionSpec as P

D = 8192
HQ = 64
HD = 128
R = 64
KD = 1024
GROUP = 8


def highest(left, right):
    return jnp.dot(left, right, precision=lax.Precision.HIGHEST, preferred_element_type=jnp.float32)


def solve_rows(rows, gram):
    lower = jnp.linalg.cholesky(gram)
    return lax.linalg.triangular_solve(lower, rows, left_side=False, lower=True, transpose_a=True)


def local(tokens, queries, key_weight, u_factor, v_factor):
    q_v = v_factor
    for turn in range(2):
        q_v = solve_rows(q_v, highest(q_v.T, q_v))
    u_rows = u_factor
    for turn in range(2):
        whole_u = lax.all_gather(u_rows, "fsdp", axis=0, tiled=True)
        u_rows = solve_rows(u_rows, highest(whole_u.T, whole_u))
    q_low = u_rows.astype(jnp.bfloat16)
    whole_x = lax.all_gather(tokens, "seq", axis=1, tiled=True)[0]
    length = whole_x.shape[0]
    slice_width = key_weight.shape[1]
    weight_piece = lax.all_gather(key_weight, "fsdp", axis=0, tiled=True)
    factor_piece = lax.all_gather(q_low, "fsdp", axis=0, tiled=True)
    base = jnp.dot(whole_x, weight_piece, preferred_element_type=jnp.float32)
    side = jnp.dot(whole_x, factor_piece, preferred_element_type=jnp.float32)
    col_start = lax.axis_index("seq") * slice_width
    v_slice = lax.dynamic_slice_in_dim(q_v, col_start, slice_width, 0)
    offset = 2.0 * highest(side, v_slice.T)
    keys = jnp.stack([base + offset, base - offset]).astype(jnp.bfloat16)
    local_kv = slice_width // HD
    query_rows = queries[0]
    query_heads = query_rows.reshape(length, local_kv, GROUP, HD).transpose(1, 2, 0, 3)
    key_heads = keys.reshape(2, length, local_kv, HD).transpose(2, 0, 1, 3)
    places = jnp.arange(length)
    causal = places[:, None] >= places[None, :]
    factor_scale = 1.0 / math.sqrt(HD)

    def one_query_head(query_one, key_one):
        scores = (
            jnp.einsum("td,npd->ntp", query_one, key_one, preferred_element_type=jnp.float32)
            * factor_scale
        )
        scores = jnp.where(causal[None], scores, -1e30)
        top = jnp.max(scores, axis=-1)
        total = jnp.sum(jnp.where(causal[None], jnp.exp(scores - top[..., None]), 0.0), axis=-1)
        return jnp.sum(top + jnp.log(total), axis=1)

    def one_key_head(pair):
        group_queries, key_one = pair
        return jnp.sum(
            lax.map(lambda query_one: one_query_head(query_one, key_one), group_queries), axis=0
        )

    partial_sums = jnp.sum(lax.map(one_key_head, (query_heads, key_heads)), axis=0)
    sums = lax.psum(partial_sums, ("fsdp", "seq"))
    losses = sums / (lax.axis_size("fsdp") * length * HQ)
    unit = math.sqrt(D * KD / R)
    update = unit * highest(u_rows, q_v.T)
    return (update, losses)


def solution(mesh):
    in_specs = (
        P("fsdp", "seq", None),
        P("fsdp", None, "seq"),
        P("fsdp", "seq"),
        P("fsdp", None),
        P(),
    )
    out_specs = (P("fsdp", None), P())
    return jax.shard_map(local, mesh=mesh, in_specs=in_specs, out_specs=out_specs, check_vma=False)
```

profile of v0, /device:TPU:1, one launch (start us, length us, event | category | flops | bytes accessed | tf_op | source)
XLA Modules:
  0.0 858.6 jit_solution(16340279235827252313)
XLA Ops:
  7.2 0.7 all-gather.6.cloned.1.call-update
  8.0 151.0 %all-gather.6.cloned.1.call-done = f32[8192,64]{1,0:T(8,128)} async-done(((f32[64,64]{1,0:T(8,128)}), f32[8192,64]{1,0:T(8,128)}) %all-gather.6.cloned.1.call-update) | async-done | bytes 2097168 | tf_op jit(solution)/shard_map/all_gather | solution.py:30
  159.0 10.4 %fusion.30 = f32[64,64]{1,0:T(8,128)S(1)} fusion(f32[8192,64]{1,0:T(8,128)} %all-gather.6.cloned.1.call-done), kind=kOutput, calls=%fused_computation.63 | convolution fusion | flops 402653184 | bytes 2113536 | tf_op jit(solution)/shard_map/dot_general | solution.py:16
  169.5 5.8 cholesky.74
  175.4 0.6 compare_reduce_fusion.3
  176.1 0.7 fusion.14
  176.7 4.9 custom-call.10
  181.9 0.7 copy.22
  182.8 137.7 %all-gather.8.cloned.1.call-done = f32[8192,64]{1,0:T(8,128)} async-done(((f32[64,64]{1,0:T(8,128)}), f32[8192,64]{1,0:T(8,128)}) %all-gather.8.cloned.1.call-update) | async-done | bytes 2097168 | tf_op jit(solution)/shard_map/all_gather | solution.py:30
  320.6 10.4 %fusion.31 = f32[64,64]{1,0:T(8,128)S(1)} fusion(f32[8192,64]{1,0:T(8,128)} %all-gather.8.cloned.1.call-done), kind=kOutput, calls=%fused_computation.64 | convolution fusion | flops 402653184 | bytes 2113536 | tf_op jit(solution)/shard_map/dot_general | solution.py:16
  331.1 5.8 cholesky.85
  337.0 0.6 compare_reduce_fusion.2
  337.6 0.7 fusion.15
  338.3 4.9 custom-call.11
  343.4 0.7 copy.27
  345.8 5.8 cholesky.96
  351.7 0.6 compare_reduce_fusion.1
  352.3 0.7 fusion.16
  353.0 4.9 custom-call.12
  358.8 5.9 cholesky.107
  364.7 0.6 compare_reduce_fusion
  365.3 0.7 fusion.17
  366.0 4.9 custom-call.13
  370.9 2.8 copy.26
  374.1 107.1 %all-gather.14.cloned.1.call-done = bf16[8192,64]{1,0:T(8,128)(2,1)} async-done(((bf16[64,64]{1,0:T(8,128)(2,1)}), bf16[8192,64]{1,0:T(8,128)(2,1)}) %all-gather.14.cloned.1.call-update) | async-done | bytes 1048592 | tf_op jit(solution)/shard_map/all_gather | solution.py:37
  481.1 88.4 %all-gather.10.cloned.1.call-done = bf16[1,512,8192]{2,1,0:T(8,128)(2,1)} async-done(((bf16[1,128,8192]{2,1,0:T(8,128)(2,1)}), bf16[1,512,8192]{2,1,0:T(8,128)(2,1)}) %all-gather.10.cloned.1.call-update) | async-done | bytes 8388624 | tf_op jit(solution)/shard_map/all_gather | solution.py:33
  569.6 6.7 fusion.9
  576.3 0.6 convolution_multiply_fusion
  576.9 139.4 %all-gather.12.cloned.1.call-done = bf16[8192,256]{1,0:T(8,128)(2,1)} async-done(((bf16[64,256]{1,0:T(8,128)(2,1)}), bf16[8192,256]{1,0:T(8,128)(2,1)}) %all-gather.12.cloned.1.call-update) | async-done | bytes 4194320 | tf_op jit(solution)/shard_map/all_gather | solution.py:36
  716.3 6.9 add_convert_fusion
  723.7 25.3 %while.26 = (s32[]{:T(128)}, f32[2,2]{1,0:T(2,128)S(1)}, bf16[2,8,512,128]{2,3,1,0:T(8,128)(2,1)}, bf16[2,2,512,128]{3,2,1,0:T(8,128)(2,1)S(1)}, s32[]{:T(128)},...) while((s32[]{:T(128)}, f32[2,2]{1,0:T(2,128)S(1)}, ...), condition=%wide.region_9.13_spmd.clone.clone, body=%wide.region_2.12_spmd.clone.clone.sunk | while | flops 138674192 | bytes 10113394 | solution.py:68
  723.7 1.3 constant_dynamic-slice_fusion.2
  725.0 0.7 copy.33
  725.8 10.4 %while.27 = (s32[]{:T(128)}, f32[8,2]{1,0:T(8,128)S(1)}, pred[512,512]{0,1:T(8,128)(4,1)S(1)}, bf16[8,512,128]{2,1,0:T(8,128)(2,1)S(1)}, bf16[2,512,128]{2,1,0:T(8,128)(2,1)S(1)}, /*index=5*/s32[]{:T(128)}, s32[]{:T(128)}) while((s32[]{:T(128)}, f32[8,2]{1,0:T(8,128)S(1)}, pred[512,512]{0,1:T(8,128)(4,1)S(1)}, ...), condition=%wide.region_7.10_spmd.clone, body=%wide.region_3.9_spmd.clone.sunk | while | flops 138412032 | bytes 5132397 | solution.py:65
  725.8 0.6 bitcast_reduce_fusion.2
  726.4 0.6 fusion.55
  727.1 0.6 bitcast_reduce_fusion.2
  727.7 0.6 fusion.55
  728.4 0.6 bitcast_reduce_fusion.2
  729.0 0.6 fusion.55
  729.7 0.6 bitcast_reduce_fusion.2
  730.3 0.6 fusion.55
  731.6 0.6 fusion.55
  732.4 0.6 bitcast_reduce_fusion.2
  732.9 0.6 fusion.55
  733.7 0.6 bitcast_reduce_fusion.2
  734.2 0.6 fusion.55
  735.0 0.6 bitcast_reduce_fusion.2
  735.5 0.6 fusion.55
  736.3 1.3 constant_dynamic-slice_fusion.2
  737.7 0.7 copy.33
  738.5 10.4 %while.27 = (s32[]{:T(128)}, f32[8,2]{1,0:T(8,128)S(1)}, pred[512,512]{0,1:T(8,128)(4,1)S(1)}, bf16[8,512,128]{2,1,0:T(8,128)(2,1)S(1)}, bf16[2,512,128]{2,1,0:T(8,128)(2,1)S(1)}, /*index=5*/s32[]{:T(128)}, s32[]{:T(128)}) while((s32[]{:T(128)}, f32[8,2]{1,0:T(8,128)S(1)}, pred[512,512]{0,1:T(8,128)(4,1)S(1)}, ...), condition=%wide.region_7.10_spmd.clone, body=%wide.region_3.9_spmd.clone.sunk | while | flops 138412032 | bytes 5132397 | solution.py:65
  738.5 0.6 bitcast_reduce_fusion.2
  739.0 0.6 fusion.55
  739.8 0.6 bitcast_reduce_fusion.2
  740.3 0.6 fusion.55
  741.7 0.6 fusion.55
  743.0 0.6 fusion.55
  744.3 0.6 fusion.55
  745.6 0.6 fusion.55
  746.9 0.6 fusion.55
  748.2 0.6 fusion.55
  749.0 1.1 convolution_multiply_fusion.1
  750.1 101.5 %psum.7 = f32[2]{0:T(128)S(1)} all-reduce(f32[2]{0:T(128)S(1)} %reduce_sum.36), channel_id=1, replica_groups=mesh['fsdp'=128,'seq'=4] {'fsdp','seq'}, use_global_device_ids=true, to_apply=%region_11.15 | all-reduce | flops 2 | bytes 16 | tf_op jit(solution)/shard_map/psum | solution.py:69
  (88 shorter events, 11.6 us)
Async XLA Ops:
  7.2 338.2 %copy-start = (f32[1024,64]{0,1:T(8,128)S(1)}, f32[1024,64]{0,1:T(8,128)}, u32[]{:S(2)}) copy-start(f32[1024,64]{0,1:T(8,128)} %param.18) | copy-start | bytes 786436
  7.2 151.8 %all-gather.6.cloned.1.call-start = ((), (), s32[]{:S(2)}) async-start(), calls=%async_computation | async-start | bytes 4227072 | tf_op jit(solution)/shard_map/all_gather | solution.py:30
  7.9 173.7 %copy-start.2 = (f32[64,64]{1,0:T(8,128)S(1)}, f32[64,64]{1,0:T(8,128)}, u32[]{:S(2)}) copy-start(f32[64,64]{1,0:T(8,128)} %param.17) | copy-start | bytes 49156
  7.9 312.6 %all-gather.8.cloned.1.call-start = ((), (), s32[]{:S(2)}) async-start(), calls=%async_computation.1 | async-start | bytes 4227072 | tf_op jit(solution)/shard_map/all_gather | solution.py:30
  182.6 298.5 %all-gather.14.cloned.1.call-start = ((), (), s32[]{:S(2)}) async-start(), calls=%async_computation.4 | async-start | bytes 2113536 | tf_op jit(solution)/shard_map/all_gather | solution.py:37
  344.2 26.7 %copy-start.1 = (bf16[1,512,2048]{2,1,0:T(8,128)(2,1)S(1)}, bf16[1,512,2048]{2,1,0:T(8,128)(2,1)}, u32[]{:S(2)}) copy-start(bf16[1,512,2048]{2,1,0:T(8,128)(2,1)} %param.15) | copy-start | bytes 6291460
  344.2 225.4 %all-gather.10.cloned.1.call-start = ((), (), s32[]{:S(2)}) async-start(), calls=%async_computation.2 | async-start | bytes 10485760 | tf_op jit(solution)/shard_map/all_gather | solution.py:33
  344.7 371.6 %all-gather.12.cloned.1.call-start = ((), (), s32[]{:S(2)}) async-start(), calls=%async_computation.3 | async-start | bytes 4227072 | tf_op jit(solution)/shard_map/all_gather | solution.py:36
Sparse Core Ops, SparseCore 0:
  11.1 147.8 all-gather.5
  182.7 137.7 all-gather.7
  344.3 136.8 all-gather.13
  483.1 86.4 all-gather.9
  572.5 143.6 all-gather.11
where the time goes:
time: 859 us
  waiting for transfers between devices  625 us (73%)
  blocking collectives  101 us (12%)
  other arithmetic  60.3 us (7%)
  matrix products  47.2 us (5%)
  between operations  14 us (2%)
  local copies, waits for them, and re-layouts  9.49 us (1%)
    all_gather x2, waiting for transfers between devices, local(): whole_u = lax.all_gather(u_rows, 'fsdp', axis=0, tiled=True)  289 us
    all_gather x1, waiting for transfers between devices, local(): weight_piece = lax.all_gather(key_weight, 'fsdp', axis=0, tiled=True)  139 us
    all_gather x1, waiting for transfers between devices, local(): factor_piece = lax.all_gather(q_low, 'fsdp', axis=0, tiled=True)  107 us
    psum x1, blocking collectives, local(): sums = lax.psum(partial_sums, ('fsdp', 'seq'))  101 us
    all_gather x1, waiting for transfers between devices, local(): whole_x = lax.all_gather(tokens, 'seq', axis=1, tiled=True)[0]  88.4 us
    another operation x12, other arithmetic, solve_rows(): lower = jnp.linalg.cholesky(gram)  26.1 us
    dot_general x6, matrix products, highest(): jnp.dot(left, right, precision=lax.Precision.HIGHEST, preferred_element_t...  23.4 us
    another operation x8, other arithmetic, solve_rows(): lax.linalg.triangular_solve(lower, rows, left_side=False, lower=True, tra...  22.2 us
  transfers between devices with their start and end apart: 5, of which 5 were waited for; matrix products, arithmetic and copies ran while one was open for 4% of the time, Pallas kernels for 0%

commit v1 on v0

--- a/solution.py
+++ b/solution.py
@@ -10,6 +10,22 @@
 R = 64
 KD = 1024
 GROUP = 8
+
+
+def gather_around(x, axis, dim):
+    ways, here, hop = (lax.axis_size(axis), lax.axis_index(axis), x.shape[dim])
+    shape = [n * ways if d == dim else n for d, n in enumerate(x.shape)]
+    full = lax.dynamic_update_slice_in_dim(jnp.zeros(shape, x.dtype), x, here * hop, axis=dim)
+    going_up = going_down = x
+    for far in range(1, ways // 2 + 1):
+        going_up = lax.ppermute(going_up, axis, [(d, (d + 1) % ways) for d in range(ways)])
+        full = lax.dynamic_update_slice_in_dim(full, going_up, (here - far) % ways * hop, axis=dim)
+        if 2 * far < ways:
+            going_down = lax.ppermute(going_down, axis, [(d, (d - 1) % ways) for d in range(ways)])
+            full = lax.dynamic_update_slice_in_dim(
+                full, going_down, (here + far) % ways * hop, axis=dim
+            )
+    return full
 
 
 def highest(left, right):
@@ -30,7 +46,7 @@
         whole_u = lax.all_gather(u_rows, "fsdp", axis=0, tiled=True)
         u_rows = solve_rows(u_rows, highest(whole_u.T, whole_u))
     q_low = u_rows.astype(jnp.bfloat16)
-    whole_x = lax.all_gather(tokens, "seq", axis=1, tiled=True)[0]
+    whole_x = gather_around(tokens, "seq", 1)[0]
     length = whole_x.shape[0]
     slice_width = key_weight.shape[1]
     weight_piece = lax.all_gather(key_weight, "fsdp", axis=0, tiled=True)

time: 859 us -> 765 us (0.89)
  waiting for transfers between devices: 625 us -> 509 us
  local copies, waits for them, and re-layouts: 9.49 us -> 22.6 us
  starting transfers between devices: 0.38 us -> 9.23 us
    all_gather x1 -> x0, waiting for transfers between devices: 88.4 us -> none  [local(): whole_x = lax.all_gather(tokens, 'seq', axis=1, tiled=True)[0]]
    all_gather x1, waiting for transfers between devices: 107 us -> 35.5 us  [local(): factor_piece = lax.all_gather(q_low, 'fsdp', axis=0, tiled=True)]
    ppermute x0 -> x3, waiting for transfers between devices: none -> 50.2 us  [the longest x2 50.2 us: gather_around(): lax.ppermute(going_up, axis, [(d, (d + 1) % ways) for d in range(ways)])]
    dynamic_update_slice x0 -> x4, local copies, waits for them, and re-layouts: none -> 9.15 us  [the longest x2 4.59 us: gather_around(): lax.dynamic_update_slice_in_dim(full, going_up, (here - far) % ways * hop...]
    ppermute x0 -> x3, starting transfers between devices: none -> 8.89 us  [the longest x2 5.27 us: gather_around(): lax.ppermute(going_up, axis, [(d, (d + 1) % ways) for d in range(ways)])]
  transfers between devices with their start and end apart: 5 -> 7, of which waited for: 5 -> 6; matrix products, arithmetic and copies ran while one was open for 4% -> 6% of each run, Pallas kernels for 0% -> 0%
where the time goes in v1:
time: 765 us; the launch traced here: 764 us
  waiting for transfers between devices  509 us (67%)
  blocking collectives  101 us (13%)
  other arithmetic  60.3 us (8%)
  matrix products  47 us (6%)
  local copies, waits for them, and re-layouts  22.6 us (3%)
  between operations  14.1 us (2%)
  starting transfers between devices  9.23 us (1%)
    all_gather x2, waiting for transfers between devices, local(): whole_u = lax.all_gather(u_rows, 'fsdp', axis=0, tiled=True)  289 us
    all_gather x1, waiting for transfers between devices, local(): weight_piece = lax.all_gather(key_weight, 'fsdp', axis=0, tiled=True)  134 us
    psum x1, blocking collectives, local(): sums = lax.psum(partial_sums, ('fsdp', 'seq'))  101 us
    ppermute x2, waiting for transfers between devices, gather_around(): lax.ppermute(going_up, axis, [(d, (d + 1) % ways) for d in range(ways)])  50.2 us
    all_gather x1, waiting for transfers between devices, local(): factor_piece = lax.all_gather(q_low, 'fsdp', axis=0, tiled=True)  35.5 us
    another operation x12, other arithmetic, solve_rows(): lower = jnp.linalg.cholesky(gram)  26.1 us
    dot_general x6, matrix products, highest(): jnp.dot(left, right, precision=lax.Precision.HIGHEST, preferred_element_t...  23.3 us
    another operation x8, other arithmetic, solve_rows(): lax.linalg.triangular_solve(lower, rows, left_side=False, lower=True, tra...  22.2 us
  transfers between devices with their start and end apart: 7, of which 6 were waited for; matrix products, arithmetic and copies ran while one was open for 6% of the time, Pallas kernels for 0%

profile of v1, /device:TPU:1, one launch (start us, length us, event | category | flops | bytes accessed | tf_op | source)
XLA Modules:
  0.0 764.5 jit_solution(15409522878872433680)
XLA Ops:
  7.2 0.7 all-gather.5.cloned.1.call-update
  8.0 151.0 %all-gather.5.cloned.1.call-done = f32[8192,64]{1,0:T(8,128)} async-done(((f32[64,64]{1,0:T(8,128)}), f32[8192,64]{1,0:T(8,128)}) %all-gather.5.cloned.1.call-update) | async-done | bytes 2097168 | tf_op jit(solution)/shard_map/all_gather | solution.py:46
  159.0 10.4 %fusion.26 = f32[64,64]{1,0:T(8,128)S(1)} fusion(f32[8192,64]{1,0:T(8,128)} %all-gather.5.cloned.1.call-done), kind=kOutput, calls=%fused_computation.63 | convolution fusion | flops 402653184 | bytes 2113536 | tf_op jit(solution)/shard_map/dot_general | solution.py:32
  169.5 5.8 cholesky.74
  175.4 0.6 compare_reduce_fusion.3
  176.1 0.7 fusion.10
  176.7 4.9 custom-call.10
  181.9 0.7 copy.22
  182.8 137.7 %all-gather.7.cloned.1.call-done = f32[8192,64]{1,0:T(8,128)} async-done(((f32[64,64]{1,0:T(8,128)}), f32[8192,64]{1,0:T(8,128)}) %all-gather.7.cloned.1.call-update) | async-done | bytes 2097168 | tf_op jit(solution)/shard_map/all_gather | solution.py:46
  320.6 10.4 %fusion.27 = f32[64,64]{1,0:T(8,128)S(1)} fusion(f32[8192,64]{1,0:T(8,128)} %all-gather.7.cloned.1.call-done), kind=kOutput, calls=%fused_computation.64 | convolution fusion | flops 402653184 | bytes 2113536 | tf_op jit(solution)/shard_map/dot_general | solution.py:32
  331.1 5.8 cholesky.85
  337.0 0.6 compare_reduce_fusion.2
  337.6 0.7 fusion.11
  338.3 4.9 custom-call.11
  343.4 0.7 copy.27
  344.2 3.1 collective-permute-start
  347.3 3.6 collective-permute-start.1
  351.5 5.8 cholesky.96
  357.4 0.6 compare_reduce_fusion.1
  358.0 0.7 fusion.12
  358.7 4.9 custom-call.12
  364.5 5.9 cholesky.107
  370.4 0.6 compare_reduce_fusion
  371.0 0.7 fusion.13
  371.7 4.9 custom-call.13
  376.6 2.6 copy.26
  379.1 4.2 squeeze.23
  383.4 1.5 bitcast_dynamic-update-slice_fusion.3
  385.3 9.3 %collective-permute-done = bf16[1,128,8192]{2,1,0:T(8,128)(2,1)} collective-permute-done((bf16[1,128,8192]{2,1,0:T(8,128)(2,1)}, bf16[1,128,8192]{2,1,0:T(8,128)(2,1)}, u32[]{:S(2)}, u32[]{:S(2)}) %collective-permute-start) | collective-permute-done | bytes 2097184 | tf_op jit(solution)/shard_map/ppermute | solution.py:21
  394.5 2.2 collective-permute-start.2
  396.7 3.1 bitcast_dynamic-update-slice_fusion.2
  399.8 3.1 bitcast_dynamic-update-slice_fusion.1
  402.9 41.0 %collective-permute-done.2 = bf16[1,128,8192]{2,1,0:T(8,128)(2,1)S(1)} collective-permute-done((bf16[1,128,8192]{2,1,0:T(8,128)(2,1)}, bf16[1,128,8192]{2,1,0:T(8,128)(2,1)S(1)}, u32[]{:S(2)}, u32[]{:S(2)}) %collective-permute-start.2) | collective-permute-done | bytes 2097184 | tf_op jit(solution)/shard_map/ppermute | solution.py:21
  443.9 1.5 bitcast_dynamic-update-slice_fusion
  445.3 35.5 %all-gather.11.cloned.1.call-done = bf16[8192,64]{1,0:T(8,128)(2,1)} async-done(((bf16[64,64]{1,0:T(8,128)(2,1)}), bf16[8192,64]{1,0:T(8,128)(2,1)}) %all-gather.11.cloned.1.call-update) | async-done | bytes 1048592 | tf_op jit(solution)/shard_map/all_gather | solution.py:53
  480.9 6.6 fusion.30
  487.5 0.6 convolution_multiply_fusion
  488.1 134.1 %all-gather.9.cloned.1.call-done = bf16[8192,256]{1,0:T(8,128)(2,1)} async-done(((bf16[64,256]{1,0:T(8,128)(2,1)}), bf16[8192,256]{1,0:T(8,128)(2,1)}) %all-gather.9.cloned.1.call-update) | async-done | bytes 4194320 | tf_op jit(solution)/shard_map/all_gather | solution.py:52
  622.3 6.9 add_convert_fusion
  629.6 25.2 %while.26 = (s32[]{:T(128)}, f32[2,2]{1,0:T(2,128)S(1)}, bf16[2,8,512,128]{2,3,1,0:T(8,128)(2,1)}, bf16[2,2,512,128]{3,2,1,0:T(8,128)(2,1)S(1)}, s32[]{:T(128)},...) while((s32[]{:T(128)}, f32[2,2]{1,0:T(2,128)S(1)}, ...), condition=%wide.region_9.13_spmd.clone.clone, body=%wide.region_2.12_spmd.clone.clone.sunk | while | flops 138674192 | bytes 10113394 | solution.py:84
  629.6 1.3 constant_dynamic-slice_fusion.2
  631.0 0.7 copy.33
  631.8 10.4 %while.27 = (s32[]{:T(128)}, f32[8,2]{1,0:T(8,128)S(1)}, pred[512,512]{0,1:T(8,128)(4,1)S(1)}, bf16[8,512,128]{2,1,0:T(8,128)(2,1)S(1)}, bf16[2,512,128]{2,1,0:T(8,128)(2,1)S(1)}, /*index=5*/s32[]{:T(128)}, s32[]{:T(128)}) while((s32[]{:T(128)}, f32[8,2]{1,0:T(8,128)S(1)}, pred[512,512]{0,1:T(8,128)(4,1)S(1)}, ...), condition=%wide.region_7.10_spmd.clone, body=%wide.region_3.0_spmd.clone.sunk | while | flops 138412032 | bytes 5132397 | solution.py:81
  632.3 0.6 fusion.54
  633.6 0.6 fusion.54
  634.9 0.6 fusion.54
  636.2 0.6 fusion.54
  637.5 0.6 fusion.54
  638.8 0.6 fusion.54
  640.1 0.6 fusion.54
  641.4 0.6 fusion.54
  642.2 1.3 constant_dynamic-slice_fusion.2
  643.6 0.7 copy.33
  644.4 10.4 %while.27 = (s32[]{:T(128)}, f32[8,2]{1,0:T(8,128)S(1)}, pred[512,512]{0,1:T(8,128)(4,1)S(1)}, bf16[8,512,128]{2,1,0:T(8,128)(2,1)S(1)}, bf16[2,512,128]{2,1,0:T(8,128)(2,1)S(1)}, /*index=5*/s32[]{:T(128)}, s32[]{:T(128)}) while((s32[]{:T(128)}, f32[8,2]{1,0:T(8,128)S(1)}, pred[512,512]{0,1:T(8,128)(4,1)S(1)}, ...), condition=%wide.region_7.10_spmd.clone, body=%wide.region_3.0_spmd.clone.sunk | while | flops 138412032 | bytes 5132397 | solution.py:81
  644.9 0.6 fusion.54
  646.2 0.6 fusion.54
  647.5 0.6 fusion.54
  648.8 0.6 fusion.54
  650.1 0.6 fusion.54
  651.4 0.6 fusion.54
  652.7 0.6 fusion.54
  654.0 0.6 fusion.54
  654.8 1.1 convolution_multiply_fusion.1
  655.9 101.5 %psum.7 = f32[2]{0:T(128)S(1)} all-reduce(f32[2]{0:T(128)S(1)} %reduce_sum.36), channel_id=1, replica_groups=mesh['fsdp'=128,'seq'=4] {'fsdp','seq'}, use_global_device_ids=true, to_apply=%region_11.15 | all-reduce | flops 2 | bytes 16 | tf_op jit(solution)/shard_map/psum | solution.py:85
  (98 shorter events, 15.5 us)
Async XLA Ops:
  7.2 343.9 %copy-start = (f32[1024,64]{0,1:T(8,128)S(1)}, f32[1024,64]{0,1:T(8,128)}, u32[]{:S(2)}) copy-start(f32[1024,64]{0,1:T(8,128)} %param.18) | copy-start | bytes 786436
  7.2 151.8 %all-gather.5.cloned.1.call-start = ((), (), s32[]{:S(2)}) async-start(), calls=%async_computation | async-start | bytes 4227072 | tf_op jit(solution)/shard_map/all_gather | solution.py:46
  7.9 173.7 %copy-start.3 = (f32[64,64]{1,0:T(8,128)S(1)}, f32[64,64]{1,0:T(8,128)}, u32[]{:S(2)}) copy-start(f32[64,64]{1,0:T(8,128)} %param.17) | copy-start | bytes 49156
  7.9 312.6 %all-gather.7.cloned.1.call-start = ((), (), s32[]{:S(2)}) async-start(), calls=%async_computation.1 | async-start | bytes 4227072 | tf_op jit(solution)/shard_map/all_gather | solution.py:46
  182.6 194.0 %copy-start.1 = (bf16[1,512,2048]{2,1,0:T(8,128)(2,1)S(1)}, bf16[1,512,2048]{2,1,0:T(8,128)(2,1)}, u32[]{:S(2)}) copy-start(bf16[1,512,2048]{2,1,0:T(8,128)(2,1)} %param.15) | copy-start | bytes 6291460
  182.6 298.2 %all-gather.11.cloned.1.call-start = ((), (), s32[]{:S(2)}) async-start(), calls=%async_computation.3 | async-start | bytes 2113536 | tf_op jit(solution)/shard_map/all_gather | solution.py:53
  344.2 278.1 %all-gather.9.cloned.1.call-start = ((), (), s32[]{:S(2)}) async-start(), calls=%async_computation.2 | async-start | bytes 4227072 | tf_op jit(solution)/shard_map/all_gather | solution.py:52
  344.2 50.3 %collective-permute-start = (bf16[1,128,8192]{2,1,0:T(8,128)(2,1)}, bf16[1,128,8192]{2,1,0:T(8,128)(2,1)}, u32[]{:S(2)}, u32[]{:S(2)}) collective-permute-start(bf16[1,128,8192]{2,1,0:T(8,128)(2,1)} %param.14), channel_id=1, source_target_pairs={{0,1},{1,2},{2,3},{3,0},{4,5},{5,6},{6,7},{7,4},{8,9},{9,10},{10,1... | collective-permute-start | bytes 6291464 | tf_op jit(solution)/shard_map/ppermute | solution.py:21
  347.3 52.5 %collective-permute-start.1 = (bf16[1,128,8192]{2,1,0:T(8,128)(2,1)}, bf16[1,128,8192]{2,1,0:T(8,128)(2,1)}, u32[]{:S(2)}, u32[]{:S(2)}) collective-permute-start(bf16[1,128,8192]{2,1,0:T(8,128)(2,1)} %param.14), channel_id=1, source_target_pairs={{0,3},{1,0},{2,1},{3,2},{4,7},{5,4},{6,5},{7,6},{8,11},{9,8},{10,9... | collective-permute-start | bytes 6291464 | tf_op jit(solution)/shard_map/ppermute | solution.py:24
  379.1 4.2 copy-start.2
  394.5 49.4 %collective-permute-start.2 = (bf16[1,128,8192]{2,1,0:T(8,128)(2,1)}, bf16[1,128,8192]{2,1,0:T(8,128)(2,1)S(1)}, u32[]{:S(2)}, u32[]{:S(2)}) collective-permute-start(bf16[1,128,8192]{2,1,0:T(8,128)(2,1)} %collective-permute-done), channel_id=1, source_target_pairs={{0,1},{1,2},{2,3},{3,0},{4,5},{5,6},{6,7},{7,4},{8,9},{9,10},{10,1... | collective-permute-start | bytes 6291464 | tf_op jit(solution)/shard_map/ppermute | solution.py:21
Sparse Core Ops, SparseCore 0:
  11.1 147.8 all-gather.4
  182.7 137.7 all-gather.6
  344.3 136.5 all-gather.10
  483.9 138.3 all-gather.8
